TPU v7x, 768 devices: a whole 4x8x12 slice. The times are simulated.
768 devices in a mesh: ctx: 384 (over z_lo, y, x, core), head: 2 (over z_hi).
Axes of the slice: x: 4, y: 8, z: 12 (z_hi: 2, z_lo: 6; z = z_hi * 6 + z_lo), core: 2. Of those that a mesh axis runs over, the one named last changes fastest.
Arguments:
- document_lengths: int32 [192], replicated, may hold values from 1 to 512, 49152 in all
- delta_query: bfloat16 [49152, 8, 128], P('ctx', 'head'), may hold values from -6 to 6
- delta_keys: bfloat16 [49152, 8, 128], P('ctx', 'head'), may hold values from -6 to 6
- delta_values: bfloat16 [49152, 16, 128], P('ctx', 'head'), may hold values from -6 to 6
- write_strength: float32 [49152, 16], P('ctx', 'head'), may hold values from 0.2 to 0.5
- log_decay: float32 [49152, 16], P('ctx', 'head'), may hold values from -0.7 to 0
- saved_state: float32 [384, 16, 128, 128], P('ctx', 'head'), may hold values from -3 to 3
- delta_cotangent: bfloat16 [49152, 16, 128], P('ctx', 'head'), may hold values from -6 to 6
- soft_query: bfloat16 [49152, 8, 256], P('ctx', 'head'), may hold values from -5 to 5
- soft_keys: bfloat16 [49152, 2, 256], P('ctx', 'head'), may hold values from -5 to 5
- soft_values: bfloat16 [49152, 2, 256], P('ctx', 'head'), may hold values from -6 to 6
- gate_logits: bfloat16 [49152, 8, 256], P('ctx', 'head'), may hold values from -8 to 8
- soft_cotangent: bfloat16 [49152, 8, 256], P('ctx', 'head'), may hold values from -6 to 6
- gate_weight: bfloat16 [2048, 8, 256], P(None, 'head'), may hold values from -0.125 to 0.125
Outputs:
- readout_grad: float32 [49152, 8, 128], P('ctx', 'head')
- address_grad: float32 [49152, 8, 128], P('ctx', 'head')
- content_grad: float32 [49152, 16, 128], P('ctx', 'head')
- strength_grad: float32 [49152, 16], P('ctx', 'head')
- decay_grad: float32 [49152, 16], P('ctx', 'head')
- query_grad: float32 [49152, 8, 256], P('ctx', 'head')
- keys_grad: float32 [49152, 2, 256], P('ctx', 'head')
- values_grad: float32 [49152, 2, 256], P('ctx', 'head')
- input_grad: float32 [49152, 2048], P(('ctx', 'head'))
Inputs may be any that keep to these rules, and one draw needn't show every extreme that they name: `document_lengths`: the lengths in tokens of 192 documents packed in order along the sequence; they sum to 49152, and the longest has exactly 512 tokens.
All inputs are finite; a program needn't handle non-finite values.
Results may differ from a plain program's by a relative error of at most 0.03.
Values may be sent and summed in bfloat16 or wider, within the bound.
No kernel may reach another device: no remote copies, remote signals or barrier semaphores. Data moves between devices by JAX's collectives and lax.ppermute only.
A program may use at most 64 MiB of HBM per device.

v0:
```python
import jax
import jax.numpy as jnp
from jax import lax
from jax.sharding import PartitionSpec as P

HOPS = 4


def shortened(x):
    return jax.tree.map(lambda a: a.astype(jnp.bfloat16) if a.dtype == jnp.float32 else a, x)


def from_behind(x, axis, by):
    peers = lax.axis_size(axis)
    pairs = [(i, i + by) for i in range(peers) if 0 <= i + by < peers]
    return lax.ppermute(x, axis, pairs)


def segment_of(positions, doc_starts):
    return jnp.sum((doc_starts[None, :] <= positions[:, None]).astype(jnp.int32), axis=1) - 1


def matmul(spec, a, b):
    return jnp.einsum(spec, a, b, precision=lax.Precision.HIGH)


def unit_lower_inverse(lower):
    n = lower.shape[-1]
    rows = jnp.arange(n)[:, None]
    cols = jnp.arange(n)[None, :]
    eye = jnp.eye(n, dtype=jnp.float32)
    first = (rows // 2 == cols // 2) & (rows % 2 == 1) & (cols % 2 == 0)
    inverse = eye - jnp.where(first, lower, 0.0)
    size = 2
    while size < n:
        mask = (rows // (2 * size) == cols // (2 * size)) & ((rows // size) % 2 == 1) & (
            (cols // size) % 2 == 0
        )
        block = jnp.where(mask, lower, 0.0)
        inverse = inverse - matmul("hij,hjk->hik", inverse, matmul("hij,hjk->hik", block, inverse))
        size *= 2
    return inverse


@jax.custom_vjp
def unit_lower_solve(lower, inverse, target):
    return matmul("hts,hsv->htv", inverse, target)


def unit_lower_solve_fwd(lower, inverse, target):
    written = matmul("hts,hsv->htv", inverse, target)
    return written, (inverse, written)


def unit_lower_solve_bwd(saved, grad):
    inverse, written = saved
    target_grad = matmul("hst,hsv->htv", inverse, grad)
    n = inverse.shape[-1]
    strict = jnp.arange(n)[:, None] > jnp.arange(n)[None, :]
    lower_grad = jnp.where(strict, -matmul("htv,hsv->hts", target_grad, written), 0.0)
    return lower_grad, jnp.zeros_like(inverse), target_grad


unit_lower_solve.defvjp(unit_lower_solve_fwd, unit_lower_solve_bwd)


def block_system(key_rows, strength, decay_rows, segment, repeat):
    unit_key = key_rows * lax.rsqrt(jnp.sum(key_rows * key_rows, axis=-1, keepdims=True) + 1e-06)
    unit_key = jnp.repeat(unit_key, repeat, axis=1)
    length = segment.shape[0]
    offsets = jnp.arange(length)
    cumulative = jnp.cumsum(decay_rows, axis=0).T
    same_doc = segment[:, None] == segment[None, :]
    causal = offsets[:, None] >= offsets[None, :]
    strictly = offsets[:, None] > offsets[None, :]
    spread = cumulative[:, :, None] - cumulative[:, None, :]
    inclusive = jnp.exp(jnp.where(same_doc & causal, spread, -jnp.inf))
    exclusive = jnp.where(strictly, inclusive, 0.0)
    key_key = jnp.einsum("thd,shd->hts", unit_key, unit_key, precision=lax.Precision.HIGH)
    return strength.T[:, :, None] * key_key * exclusive


def delta_block(
    queries, key_rows, value_rows, strength, decay_rows, start_state, segment, continued, inverse
):
    head_size = queries.shape[-1]
    repeat = value_rows.shape[1] // queries.shape[1]
    highest = lax.Precision.HIGH
    unit_query = (
        queries
        * lax.rsqrt(jnp.sum(queries * queries, axis=-1, keepdims=True) + 1e-06)
        * head_size ** (-0.5)
    )
    unit_key = key_rows * lax.rsqrt(jnp.sum(key_rows * key_rows, axis=-1, keepdims=True) + 1e-06)
    unit_query = jnp.repeat(unit_query, repeat, axis=1)
    unit_key = jnp.repeat(unit_key, repeat, axis=1)
    length = segment.shape[0]
    offsets = jnp.arange(length)
    cumulative = jnp.cumsum(decay_rows, axis=0).T
    same_doc = segment[:, None] == segment[None, :]
    causal = offsets[:, None] >= offsets[None, :]
    strictly = offsets[:, None] > offsets[None, :]
    spread = cumulative[:, :, None] - cumulative[:, None, :]
    inclusive = jnp.exp(jnp.where(same_doc & causal, spread, -jnp.inf))
    exclusive = jnp.where(strictly, inclusive, 0.0)
    carried = jnp.exp(cumulative) * continued.astype(jnp.float32)[None, :]
    key_key = jnp.einsum("thd,shd->hts", unit_key, unit_key, precision=highest)
    query_key = jnp.einsum("thd,shd->hts", unit_query, unit_key, precision=highest)
    strength_heads = strength.T
    system = jnp.eye(length, dtype=jnp.float32) + strength_heads[:, :, None] * key_key * exclusive
    recalled = jnp.einsum("thk,hvk->htv", unit_key, start_state, precision=highest)
    target = strength_heads[:, :, None] * (
        value_rows.transpose(1, 0, 2) - carried[:, :, None] * recalled
    )
    written = unit_lower_solve(system - jnp.eye(length, dtype=jnp.float32), inverse, target)
    readout = carried[:, :, None] * jnp.einsum(
        "thk,hvk->htv", unit_query, start_state, precision=highest
    )
    readout = readout + jnp.einsum(
        "hts,hsv->htv", query_key * inclusive, written, precision=highest
    )
    last_doc = segment == segment[-1]
    fading = jnp.exp(jnp.where(last_doc[None, :], cumulative[:, -1:] - cumulative, -jnp.inf))
    final_state = carried[:, -1][:, None, None] * start_state
    final_state = final_state + jnp.einsum(
        "htv,thk->hvk", written * fading[:, :, None], unit_key, precision=highest
    )
    return (readout.transpose(1, 0, 2), final_state)


def carry_back(incoming, mapping):
    return jnp.einsum("hvk,hjk->hvj", incoming, mapping, precision=lax.Precision.HIGH)


def shards(
    document_lengths,
    delta_query,
    delta_keys,
    delta_values,
    write_strength,
    log_decay,
    saved_state,
    delta_cotangent,
    soft_query,
    soft_keys,
    soft_values,
    gate_logits,
    soft_cotangent,
    gate_weight,
):
    length = delta_query.shape[0]
    block_index = lax.axis_index("ctx")
    offsets = jnp.arange(length, dtype=jnp.int32)
    doc_starts = jnp.cumsum(document_lengths) - document_lengths
    positions = block_index * length + offsets
    segment = segment_of(positions, doc_starts)
    before = segment_of(positions[:1] - 1, doc_starts)
    continued = segment == before[0]

    local_pair = jnp.stack([soft_keys, soft_values])
    arrived = [local_pair] + [from_behind(local_pair, "ctx", d) for d in range(1, HOPS + 1)]
    window_pair = jnp.concatenate(arrived[::-1], axis=1)

    queries = delta_query.astype(jnp.float32)
    key_rows = delta_keys.astype(jnp.float32)
    value_rows = delta_values.astype(jnp.float32)
    repeat = value_rows.shape[1] // queries.shape[1]
    inverse = lax.stop_gradient(
        unit_lower_inverse(block_system(key_rows, write_strength, log_decay, segment, repeat))
    )
    inverse, window_pair = lax.optimization_barrier((inverse, window_pair))

    kv_heads = soft_keys.shape[1]
    width = soft_keys.shape[2]
    group = soft_query.shape[1] // kv_heads
    score_scale = width ** (-0.5)
    key_positions = (block_index - HOPS) * length + jnp.arange((HOPS + 1) * length, dtype=jnp.int32)
    key_segment = segment_of(key_positions, doc_starts)
    keep = (segment[:, None] == key_segment[None, :]) & (
        key_positions[None, :] <= positions[:, None]
    )
    queries_four = soft_query.reshape(length, kv_heads, group, width)
    scores = (
        jnp.einsum(
            "qkgd,tkd->kgqt", queries_four, window_pair[0], preferred_element_type=jnp.float32
        )
        * score_scale
    )
    scores = jnp.where(keep, scores, -jnp.inf)
    peak = jnp.max(scores, axis=-1, keepdims=True)
    log_total = peak + jnp.log(jnp.sum(jnp.exp(scores - peak), axis=-1, keepdims=True))
    weights = jnp.exp(scores - log_total)
    rounded = weights.astype(jnp.bfloat16)
    output = jnp.einsum(
        "kgqt,tkd->qkgd", rounded, window_pair[1], preferred_element_type=jnp.float32
    )
    gate_open = jax.nn.sigmoid(gate_logits.astype(jnp.float32)).reshape(
        length, kv_heads, group, width
    )
    upstream = soft_cotangent.astype(jnp.float32).reshape(length, kv_heads, group, width)
    slope = (
        (upstream * output * gate_open * (1.0 - gate_open))
        .astype(jnp.bfloat16)
        .reshape(length, kv_heads * group, width)
    )
    gate_full = lax.dot_general(
        slope, gate_weight, (((1, 2), (1, 2)), ((), ())), preferred_element_type=jnp.float32
    )
    gate_part = gate_full.astype(jnp.bfloat16)
    gate_full, gate_part, inverse, queries, key_rows, value_rows = lax.optimization_barrier(
        (gate_full, gate_part, inverse, queries, key_rows, value_rows)
    )
    half = gate_part.shape[0] // 2
    head_index = lax.axis_index("head")
    kept = lax.dynamic_slice_in_dim(gate_full, head_index * half, half, 0)
    sent = lax.dynamic_slice_in_dim(gate_part, (1 - head_index) * half, half, 0)
    received = lax.ppermute(sent, "head", [(0, 1), (1, 0)])

    start_state = saved_state[0]
    cotangent = delta_cotangent.astype(jnp.float32)

    def forward_state(state_in):
        return delta_block(
            queries,
            key_rows,
            value_rows,
            write_strength,
            log_decay,
            state_in,
            segment,
            continued,
            inverse,
        )

    unused_state, state_pullback = jax.vjp(forward_state, start_state)
    own_part = state_pullback((cotangent, jnp.zeros_like(start_state)))[0]
    identity = jnp.broadcast_to(
        jnp.eye(start_state.shape[-1], dtype=jnp.float32), start_state.shape
    )
    transfer = delta_block(
        queries,
        key_rows,
        jnp.zeros_like(value_rows),
        write_strength,
        log_decay,
        identity,
        segment,
        continued,
        inverse,
    )[1]
    gathered = own_part
    incoming = own_part
    for step_index in range(HOPS):
        incoming = from_behind(shortened(gathered), "ctx", -1).astype(gathered.dtype)
        gathered = own_part + carry_back(incoming, transfer)

    received, incoming = lax.optimization_barrier((received, incoming))
    input_grad = kept + received.astype(jnp.float32)

    def forward(queries_in, keys_in, values_in, strength_in, decay_in):
        return delta_block(
            queries_in,
            keys_in,
            values_in,
            strength_in,
            decay_in,
            start_state,
            segment,
            continued,
            inverse,
        )

    unused, pullback = jax.vjp(forward, queries, key_rows, value_rows, write_strength, log_decay)
    readout_grad, address_grad, content_grad, strength_grad, decay_grad = pullback(
        (cotangent, incoming)
    )

    back = (upstream * gate_open).astype(jnp.bfloat16)
    row_dot = jnp.sum(back.astype(jnp.float32) * output, axis=-1).transpose(1, 2, 0)[..., None]
    dprob = jnp.einsum("qkgd,tkd->kgqt", back, window_pair[1], preferred_element_type=jnp.float32)
    dscore = (weights * (dprob - row_dot)).astype(jnp.bfloat16)
    query_grad = (
        jnp.einsum("kgqt,tkd->qkgd", dscore, window_pair[0], preferred_element_type=jnp.float32)
        * score_scale
    )
    query_grad = query_grad.reshape(length, kv_heads * group, width)
    key_part = (
        jnp.einsum("kgqt,qkgd->tkd", dscore, queries_four, preferred_element_type=jnp.float32)
        * score_scale
    )
    value_part = jnp.einsum("kgqt,qkgd->tkd", rounded, back, preferred_element_type=jnp.float32)
    returned = jnp.stack([key_part, value_part])

    def slab(distance):
        return returned[:, (HOPS - distance) * length : (HOPS - distance + 1) * length]

    summed = slab(0)
    for distance in range(1, HOPS + 1):
        summed = summed + from_behind(
            slab(distance).astype(jnp.bfloat16), "ctx", -distance
        ).astype(summed.dtype)
    return (
        readout_grad,
        address_grad,
        content_grad,
        strength_grad,
        decay_grad,
        query_grad,
        summed[0],
        summed[1],
        input_grad,
    )


def solution(mesh):
    placed = (
        P(),
        P("ctx", "head", None),
        P("ctx", "head", None),
        P("ctx", "head", None),
        P("ctx", "head"),
        P("ctx", "head"),
        P("ctx", "head", None, None),
        P("ctx", "head", None),
        P("ctx", "head", None),
        P("ctx", "head", None),
        P("ctx", "head", None),
        P("ctx", "head", None),
        P("ctx", "head", None),
        P(None, "head", None),
    )
    return jax.shard_map(
        shards,
        mesh=mesh,
        in_specs=placed,
        out_specs=(
            P("ctx", "head", None),
            P("ctx", "head", None),
            P("ctx", "head", None),
            P("ctx", "head"),
            P("ctx", "head"),
            P("ctx", "head", None),
            P("ctx", "head", None),
            P("ctx", "head", None),
            P(("ctx", "head"), None),
        ),
        check_vma=False,
    )
```

profile of v0, /device:TPU:65, one launch (start us, length us, event | category | flops | bytes accessed | tf_op | source)
XLA Modules:
  0.0 152.3 jit_solution(17004146863409889160)
XLA Ops:
  0.7 1.6 %pad_maximum_fusion.1 = bf16[2,128,1,256]{3,1,2,0:T(8,128)(2,1)} fusion(bf16[1,128,1,256]{3,1,2,0:T(8,128)(2,1)} %bitcast.302, bf16[1,128,1,256]{3,1,2,0:T(8,128)(2,1)} %bitcast.304), kind=kLoop, calls=%fused_computation.203 | loop fusion | flops 65536 | bytes 262144 | tf_op jit(solution)/shard_map/stack | solution.py:160
  2.3 3.7 %collective-permute-start.3 = (bf16[2,128,1,256]{3,1,2,0:T(8,128)(2,1)}, bf16[2,128,1,256]{3,1,2,0:T(8,128)(2,1)}, u32[]{:S(2)}, u32[]{:S(2)}) collective-permute-start(bf16[2,128,1,256]{3,1,2,0:T(8,128)(2,1)} %pad_maximum_fusion.1), channel_id=1, source_target_pairs={{0,2},{2,4},{4,6},{6,8},{8,10},{10,12},{12,14},{14,16},{16,18},{18... | collective-permute-start | bytes 393224 | tf_op jit(solution)/shard_map/ppermute | solution.py:16
  5.9 3.1 %collective-permute-start.2 = (bf16[2,128,1,256]{3,1,2,0:T(8,128)(2,1)}, bf16[2,128,1,256]{3,1,2,0:T(8,128)(2,1)}, u32[]{:S(2)}, u32[]{:S(2)}) collective-permute-start(bf16[2,128,1,256]{3,1,2,0:T(8,128)(2,1)} %pad_maximum_fusion.1), channel_id=1, source_target_pairs={{0,4},{2,6},{4,8},{6,10},{8,12},{10,14},{12,16},{14,18},{16,20},{1... | collective-permute-start | bytes 393224 | tf_op jit(solution)/shard_map/ppermute | solution.py:16
  9.1 3.4 %collective-permute-start.1 = (bf16[2,128,1,256]{3,1,2,0:T(8,128)(2,1)}, bf16[2,128,1,256]{3,1,2,0:T(8,128)(2,1)}, u32[]{:S(2)}, u32[]{:S(2)}) collective-permute-start(bf16[2,128,1,256]{3,1,2,0:T(8,128)(2,1)} %pad_maximum_fusion.1), channel_id=1, source_target_pairs={{0,6},{2,8},{4,10},{6,12},{8,14},{10,16},{12,18},{14,20},{16,22},{... | collective-permute-start | bytes 393224 | tf_op jit(solution)/shard_map/ppermute | solution.py:16
  12.5 3.4 %collective-permute-start = (bf16[2,128,1,256]{3,1,2,0:T(8,128)(2,1)}, bf16[2,128,1,256]{3,1,2,0:T(8,128)(2,1)}, u32[]{:S(2)}, u32[]{:S(2)}) collective-permute-start(bf16[2,128,1,256]{3,1,2,0:T(8,128)(2,1)} %pad_maximum_fusion.1), channel_id=1, source_target_pairs={{0,8},{2,10},{4,12},{6,14},{8,16},{10,18},{12,20},{14,22},{16,24},... | collective-permute-start | bytes 393224 | tf_op jit(solution)/shard_map/ppermute | solution.py:16
  16.1 0.7 pad_bitcast_fusion
  17.5 1.3 fusion.150
  19.8 0.8 copy.326
  22.6 0.9 compare_and_fusion
  23.4 1.0 copy.330
  25.0 0.7 fusion.20
  31.1 0.8 copy_convert_fusion
  31.9 1.3 fusion.32
  33.2 0.9 copy.335
  34.1 0.9 copy.329
  35.0 0.9 constant_dynamic-update-slice_fusion.4
  36.0 0.9 constant_dynamic-update-slice_fusion.3
  36.9 0.9 constant_dynamic-update-slice_fusion.2
  37.8 0.9 constant_dynamic-update-slice_fusion.1
  38.8 1.5 fusion.178
  40.6 1.0 fusion.38
  41.6 1.3 convolution_bitcast_fusion.1
  43.0 2.7 %fusion.179 = (bf16[128,2048]{1,0:T(8,128)(2,1)}, f32[128,2048]{1,0:T(8,128)}) fusion(bf16[2048,4,256]{2,1,0:T(4,128)(2,1)S(1)} %copy-done.41, f32[128,1,4,256]{0,3,2,1:T(8,128)S(1)} %get-tuple-element.122, bf16[128,4,256]{0,2,1:T(8,128)(2,1)S(1)} %copy-done.34, bf16[128,4,256]{0,2,1:T(8,128)(2,1)S(1)} %copy-done.32), kind=kOutput, calls=%fused_computation.335 | convolution fusion | flops 538443776 | bytes 6815744 | tf_op jit(solution)/shard_map/dot_general | solution.py:206
  46.7 0.7 fusion.16
  48.6 0.7 copy-done.17
  49.3 0.9 fusion.52
  51.3 1.0 multiply_multiply_fusion
  53.0 0.8 convolution_add_fusion.2
  55.0 0.8 fusion.18
  56.4 3.3 %collective-permute-start.5 = (bf16[8,128,128]{2,1,0:T(8,128)(2,1)S(1)}, bf16[8,128,128]{2,1,0:T(8,128)(2,1)S(1)}, u32[]{:S(2)}, u32[]{:S(2)}) collective-permute-start(bf16[8,128,128]{2,1,0:T(8,128)(2,1)S(1)} %get-tuple-element.114), channel_id=1, source_target_pairs={{2,0},{4,2},{6,4},{8,6},{10,8},{12,10},{14,12},{16,14},{18,16},{20... | collective-permute-start | bytes 786440 | tf_op jit(solution)/shard_map/ppermute | solution.py:16
  60.8 0.8 fusion.177
  61.5 1.2 fusion.14
  62.8 1.4 collective-permute-done.5
  64.2 1.2 fusion.26
  65.4 4.8 %collective-permute-start.6 = (bf16[8,128,128]{2,1,0:T(8,128)(2,1)}, bf16[8,128,128]{2,1,0:T(8,128)(2,1)}, u32[]{:S(2)}, u32[]{:S(2)}) collective-permute-start(bf16[8,128,128]{2,1,0:T(8,128)(2,1)} %fusion.26), channel_id=1, source_target_pairs={{2,0},{4,2},{6,4},{8,6},{10,8},{12,10},{14,12},{16,14},{18,16},{20... | collective-permute-start | bytes 786440 | tf_op jit(solution)/shard_map/ppermute | solution.py:16
  70.3 0.7 constant_dynamic-slice_fusion
  71.0 2.0 %copy.384 = f32[128,4,256]{2,1,0:T(4,128)} copy(f32[128,4,256]{0,2,1:T(8,128)} %fusion.14) | data formatting | bytes 1048576
  73.0 14.1 %collective-permute-start.4 = (bf16[64,2048]{1,0:T(8,128)(2,1)}, bf16[64,2048]{1,0:T(8,128)(2,1)S(1)}, u32[]{:S(2)}, u32[]{:S(2)}) collective-permute-start(bf16[64,2048]{1,0:T(8,128)(2,1)} %constant_dynamic-slice_fusion), channel_id=1, source_target_pairs={{0,1},{1,0},{2,3},{3,2},{4,5},{5,4},{6,7},{7,6},{8,9},{9,8},{10,11... | collective-permute-start | bytes 786440 | tf_op jit(solution)/shard_map/ppermute | solution.py:217
  87.1 1.8 %copy.380 = f32[128,4,128]{2,1,0:T(4,128)} copy(f32[128,4,128]{2,0,1:T(8,128)} %get-tuple-element.100) | data formatting | bytes 524288
  89.0 8.3 %collective-permute-start.9 = (bf16[2,128,1,256]{3,1,2,0:T(8,128)(2,1)}, bf16[2,128,1,256]{3,1,2,0:T(8,128)(2,1)S(1)}, u32[]{:S(2)}, u32[]{:S(2)}) collective-permute-start(bf16[2,128,1,256]{3,1,2,0:T(8,128)(2,1)} %get-tuple-element.93), channel_id=1, source_target_pairs={{2,0},{4,2},{6,4},{8,6},{10,8},{12,10},{14,12},{16,14},{18,16},{20... | collective-permute-start | bytes 393224 | tf_op jit(solution)/shard_map/ppermute | solution.py:16
  97.3 1.9 %collective-permute-start.12 = (bf16[2,128,1,256]{3,1,2,0:T(8,128)(2,1)}, bf16[2,128,1,256]{3,1,2,0:T(8,128)(2,1)S(1)}, u32[]{:S(2)}, u32[]{:S(2)}) collective-permute-start(bf16[2,128,1,256]{3,1,2,0:T(8,128)(2,1)} %get-tuple-element.94), channel_id=1, source_target_pairs={{8,0},{10,2},{12,4},{14,6},{16,8},{18,10},{20,12},{22,14},{24,16},... | collective-permute-start | bytes 393224 | tf_op jit(solution)/shard_map/ppermute | solution.py:16
  99.2 1.9 %collective-permute-start.11 = (bf16[2,128,1,256]{3,1,2,0:T(8,128)(2,1)}, bf16[2,128,1,256]{3,1,2,0:T(8,128)(2,1)S(1)}, u32[]{:S(2)}, u32[]{:S(2)}) collective-permute-start(bf16[2,128,1,256]{3,1,2,0:T(8,128)(2,1)} %get-tuple-element.95), channel_id=1, source_target_pairs={{6,0},{8,2},{10,4},{12,6},{14,8},{16,10},{18,12},{20,14},{22,16},{... | collective-permute-start | bytes 393224 | tf_op jit(solution)/shard_map/ppermute | solution.py:16
  101.1 1.7 %fusion.29 = f32[8,128]{1,0:T(8,128)S(1)} fusion(f32[128,8,128]{2,0,1:T(8,128)S(1)} %bitcast.283, f32[1,8,128,128]{3,2,1,0:T(8,128)S(1)} %copy-done.1, bf16[128,8,128]{2,1,0:T(8,128)(2,1)} %param.21), kind=kOutput, calls=%fused_computation.64 | convolution fusion | flops 101055488 | bytes 1314816 | tf_op jit(solution)/shard_map/jvp(thk,hvk->htv)/dot_general | solution.py:116
  102.9 1.5 fusion.27
  104.4 3.8 %collective-permute-start.7 = (bf16[8,128,128]{2,1,0:T(8,128)(2,1)S(1)}, bf16[8,128,128]{2,1,0:T(8,128)(2,1)S(1)}, u32[]{:S(2)}, u32[]{:S(2)}) collective-permute-start(bf16[8,128,128]{2,1,0:T(8,128)(2,1)S(1)} %fusion.27), channel_id=1, source_target_pairs={{2,0},{4,2},{6,4},{8,6},{10,8},{12,10},{14,12},{16,14},{18,16},{20... | collective-permute-start | bytes 786440 | tf_op jit(solution)/shard_map/ppermute | solution.py:16
  108.1 1.5 fusion.182
  109.6 2.6 %collective-permute-done.7 = bf16[8,128,128]{2,1,0:T(8,128)(2,1)S(1)} collective-permute-done((bf16[8,128,128]{2,1,0:T(8,128)(2,1)S(1)}, bf16[8,128,128]{2,1,0:T(8,128)(2,1)S(1)}, u32[]{:S(2)}, u32[]{:S(2)}) %collective-permute-start.7) | collective-permute-done | bytes 262176 | tf_op jit(solution)/shard_map/ppermute | solution.py:16
  112.2 10.3 %collective-permute-start.10 = (bf16[2,128,1,256]{3,1,2,0:T(8,128)(2,1)S(1)}, bf16[2,128,1,256]{3,1,2,0:T(8,128)(2,1)S(1)}, u32[]{:S(2)}, u32[]{:S(2)}) collective-permute-start(bf16[2,128,1,256]{3,1,2,0:T(8,128)(2,1)S(1)} %copy-done.40), channel_id=1, source_target_pairs={{4,0},{6,2},{8,4},{10,6},{12,8},{14,10},{16,12},{18,14},{20,16},{2... | collective-permute-start | bytes 393224 | tf_op jit(solution)/shard_map/ppermute | solution.py:16
  123.0 2.1 %collective-permute-start.8 = (bf16[8,128,128]{2,1,0:T(8,128)(2,1)S(1)}, bf16[8,128,128]{2,1,0:T(8,128)(2,1)S(1)}, u32[]{:S(2)}, u32[]{:S(2)}) collective-permute-start(bf16[8,128,128]{2,1,0:T(8,128)(2,1)S(1)} %fusion.28), channel_id=1, source_target_pairs={{2,0},{4,2},{6,4},{8,6},{10,8},{12,10},{14,12},{16,14},{18,16},{20... | collective-permute-start | bytes 786440 | tf_op jit(solution)/shard_map/ppermute | solution.py:16
  125.4 0.8 copy.386
  126.2 0.8 copy.385
  126.9 3.8 %collective-permute-done.8 = bf16[8,128,128]{2,1,0:T(8,128)(2,1)S(1)} collective-permute-done((bf16[8,128,128]{2,1,0:T(8,128)(2,1)S(1)}, bf16[8,128,128]{2,1,0:T(8,128)(2,1)S(1)}, u32[]{:S(2)}, u32[]{:S(2)}) %collective-permute-start.8) | collective-permute-done | bytes 262176 | tf_op jit(solution)/shard_map/ppermute | solution.py:16
  131.0 1.5 multiply_reduce_fusion.1
  132.5 2.5 %bitcast_multiply_fusion = (f32[128,8,128]{0,2,1:T(8,128)}, f32[8,128,128]{1,2,0:T(8,128)}) fusion(f32[128,8]{0,1:T(8,128)S(1)} %copy-done.23, f32[8,128,128]{2,1,0:T(8,128)S(1)} %convolution_subtract_fusion, f32[8,128,128]{1,2,0:T(8,128)} %copy-done.16, f32[8,128,128]{1,2,0:T(8,128)} %get-tuple-element.120, f32[8,128]{1,0:T(8,128)S(1)} %get-tuple-element.103), kind=kOutput, calls=%fused_computation.79 | convolution fusion | flops 101056512 | bytes 2629632 | tf_op jit(solution)/shard_map/transpose(jvp(hst,hsv->htv))/dot_general | solution.py:115
  135.1 2.0 %copy.382 = f32[128,8,128]{2,1,0:T(8,128)} copy(f32[128,8,128]{0,2,1:T(8,128)} %get-tuple-element.116) | data formatting | bytes 1048576
  137.4 2.1 %copy.356 = f32[8,128,128]{2,1,0:T(8,128)} copy(f32[8,128,128]{1,2,0:T(8,128)} %get-tuple-element.117) | data formatting | bytes 1048576 | tf_op jit(solution)/shard_map/transpose(jvp(hst,hsv->htv))/dot_general | solution.py:115
  139.5 2.0 %convolution_bitcast_fusion.7 = f32[128,8,128]{0,2,1:T(8,128)S(1)} fusion(f32[1,8,128,128]{3,2,1,0:T(8,128)S(1)} %copy-done.1, f32[8,128,128]{2,1,0:T(8,128)} %copy.356, f32[8,128]{1,0:T(8,128)S(1)} %bitcast.298, f32[8,128]{1,0:T(8,128)S(1)} %get-tuple-element.104), kind=kOutput, calls=%fused_computation.54 | convolution fusion | flops 101056512 | bytes 1581056 | tf_op jit(solution)/shard_map/transpose(jvp(thk,hvk->htv))/dot_general | solution.py:111
  141.6 3.0 %multiply_select_fusion = (f32[8,128,128]{2,1,0:T(8,128)S(1)}, f32[8,128]{1,0:T(8,128)S(1)}, f32[8,128]{1,0:T(8,128)S(1)}, f32[8,128]{1,0:T(8,128)S(1)}, f32[8,128,128]{2,1,0:T(8,128)S(1)}) fusion(f32[8,128,128]{2,1,0:T(8,128)} %fusion.182, f32[8,128,128]{2,1,0:T(8,128)} %copy-done.15, f32[8,128,128]{2,1,0:T(8,128)S(1)} %copy-done.5, ...), kind=kOutput, calls=%fused_computation.90 | convolution fusion | flops 103674880 | bytes 5300224 | tf_op jit(solution)/shard_map/transpose(jvp(htv,hsv->hts))/dot_general | solution.py:115
  145.1 0.8 fusion.24
  145.9 0.9 fusion.22
  146.8 0.9 bitcast_reduce_fusion.1
  148.1 0.8 copy.381
  149.1 1.1 reduce_window_sum.44
  151.5 0.8 convert_add_fusion
  (193 shorter events, 19.2 us)
Async XLA Ops:
  0.6 38.2 %copy-start = (bf16[128,4,256]{2,1,0:T(4,128)(2,1)S(1)}, bf16[128,4,256]{2,1,0:T(4,128)(2,1)}, u32[]{:S(2)}) copy-start(bf16[128,4,256]{2,1,0:T(4,128)(2,1)} %param.22) | copy-start | bytes 786436
  0.7 24.0 %copy-start.38 = (bf16[128,4,128]{2,1,0:T(4,128)(2,1)S(1)}, bf16[128,4,128]{2,1,0:T(4,128)(2,1)}, u32[]{:S(2)}) copy-start(bf16[128,4,128]{2,1,0:T(4,128)(2,1)} %param.15) | copy-start | bytes 393220
  2.3 35.6 %collective-permute-start.3 = (bf16[2,128,1,256]{3,1,2,0:T(8,128)(2,1)}, bf16[2,128,1,256]{3,1,2,0:T(8,128)(2,1)}, u32[]{:S(2)}, u32[]{:S(2)}) collective-permute-start(bf16[2,128,1,256]{3,1,2,0:T(8,128)(2,1)} %pad_maximum_fusion.1), channel_id=1, source_target_pairs={{0,2},{2,4},{4,6},{6,8},{8,10},{10,12},{12,14},{14,16},{16,18},{18... | collective-permute-start | bytes 393224 | tf_op jit(solution)/shard_map/ppermute | solution.py:16
  5.9 30.9 %collective-permute-start.2 = (bf16[2,128,1,256]{3,1,2,0:T(8,128)(2,1)}, bf16[2,128,1,256]{3,1,2,0:T(8,128)(2,1)}, u32[]{:S(2)}, u32[]{:S(2)}) collective-permute-start(bf16[2,128,1,256]{3,1,2,0:T(8,128)(2,1)} %pad_maximum_fusion.1), channel_id=1, source_target_pairs={{0,4},{2,6},{4,8},{6,10},{8,12},{10,14},{12,16},{14,18},{16,20},{1... | collective-permute-start | bytes 393224 | tf_op jit(solution)/shard_map/ppermute | solution.py:16
  9.1 26.9 %collective-permute-start.1 = (bf16[2,128,1,256]{3,1,2,0:T(8,128)(2,1)}, bf16[2,128,1,256]{3,1,2,0:T(8,128)(2,1)}, u32[]{:S(2)}, u32[]{:S(2)}) collective-permute-start(bf16[2,128,1,256]{3,1,2,0:T(8,128)(2,1)} %pad_maximum_fusion.1), channel_id=1, source_target_pairs={{0,6},{2,8},{4,10},{6,12},{8,14},{10,16},{12,18},{14,20},{16,22},{... | collective-permute-start | bytes 393224 | tf_op jit(solution)/shard_map/ppermute | solution.py:16
  12.5 22.5 %collective-permute-start = (bf16[2,128,1,256]{3,1,2,0:T(8,128)(2,1)}, bf16[2,128,1,256]{3,1,2,0:T(8,128)(2,1)}, u32[]{:S(2)}, u32[]{:S(2)}) collective-permute-start(bf16[2,128,1,256]{3,1,2,0:T(8,128)(2,1)} %pad_maximum_fusion.1), channel_id=1, source_target_pairs={{0,8},{2,10},{4,12},{6,14},{8,16},{10,18},{12,20},{14,22},{16,24},... | collective-permute-start | bytes 393224 | tf_op jit(solution)/shard_map/ppermute | solution.py:16
  22.6 2.4 %copy-start.23 = (f32[128,8]{0,1:T(8,128)S(1)}, f32[128,8]{0,1:T(8,128)}, u32[]{:S(2)}) copy-start(f32[128,8]{0,1:T(8,128)} %param.18) | copy-start | bytes 12292
  30.1 1.0 copy-start.27
  30.5 1.4 copy-start.1
  30.5 1.4 copy-start.6
  31.1 2.1 %copy-start.30 = (bf16[128,4,256]{2,1,0:T(4,128)(2,1)S(1)}, bf16[128,4,256]{2,1,0:T(4,128)(2,1)}, u32[]{:S(2)}) copy-start(bf16[128,4,256]{2,1,0:T(4,128)(2,1)} %param.25) | copy-start | bytes 786436
  31.9 2.2 %copy-start.31 = (bf16[128,4,256]{2,1,0:T(4,128)(2,1)S(1)}, bf16[128,4,256]{2,1,0:T(4,128)(2,1)}, u32[]{:S(2)}) copy-start(bf16[128,4,256]{2,1,0:T(4,128)(2,1)} %param.26) | copy-start | bytes 786436
  33.2 5.6 %copy-start.36 = (bf16[128,1,256]{2,0,1:T(8,128)(2,1)S(1)}, bf16[128,1,256]{2,0,1:T(8,128)(2,1)}, u32[]{:S(2)}) copy-start(bf16[128,1,256]{2,0,1:T(8,128)(2,1)} %param.24) | copy-start | bytes 196612
  33.2 5.6 %copy-start.37 = (bf16[128,1,256]{2,0,1:T(8,128)(2,1)S(1)}, bf16[128,1,256]{2,0,1:T(8,128)(2,1)}, u32[]{:S(2)}) copy-start(bf16[128,1,256]{2,0,1:T(8,128)(2,1)} %param.23) | copy-start | bytes 196612
  33.2 12.5 %copy-start.7 = (f32[128,4,128]{0,2,1:T(8,128)}, f32[128,4,128]{0,2,1:T(8,128)S(1)}, u32[]{:S(2)}) copy-start(f32[128,4,128]{0,2,1:T(8,128)S(1)} %convert_element_type.111) | copy-start | bytes 786436
  38.8 1.7 %copy-start.24 = (bf16[2,640,1,256]{3,1,2,0:T(8,128)(2,1)}, bf16[2,640,1,256]{3,1,2,0:T(8,128)(2,1)S(1)}, u32[]{:S(2)}) copy-start(bf16[2,640,1,256]{3,1,2,0:T(8,128)(2,1)S(1)} %constant_dynamic-update-slice_fusion) | copy-start | bytes 1966084
  38.8 1.7 %copy-start.32 = (bf16[128,4,256]{0,2,1:T(8,128)(2,1)S(1)}, bf16[128,4,256]{0,2,1:T(8,128)(2,1)}, u32[]{:S(2)}) copy-start(bf16[128,4,256]{0,2,1:T(8,128)(2,1)} %copy.335) | copy-start | bytes 786436
  38.8 1.7 %copy-start.34 = (bf16[128,4,256]{0,2,1:T(8,128)(2,1)S(1)}, bf16[128,4,256]{0,2,1:T(8,128)(2,1)}, u32[]{:S(2)}) copy-start(bf16[128,4,256]{0,2,1:T(8,128)(2,1)} %copy.329) | copy-start | bytes 786436
  40.3 1.3 copy-start.21
  40.6 2.4 %copy-start.41 = (bf16[2048,4,256]{2,1,0:T(4,128)(2,1)S(1)}, bf16[2048,4,256]{2,1,0:T(4,128)(2,1)}, u32[]{:S(2)}) copy-start(bf16[2048,4,256]{2,1,0:T(4,128)(2,1)} %param.27) | copy-start | bytes 12582916
  46.0 1.4 copy-start.22
  46.0 1.5 copy-start.25
  46.0 1.5 copy-start.33
  46.0 1.6 %copy-start.35 = (bf16[128,4,256]{0,2,1:T(8,128)(2,1)S(1)}, bf16[128,4,256]{0,2,1:T(8,128)(2,1)}, u32[]{:S(2)}) copy-start(bf16[128,4,256]{0,2,1:T(8,128)(2,1)} %copy.329) | copy-start | bytes 786436
  46.0 1.6 %copy-start.42 = (f32[128,4]{0,1:T(4,128)S(1)}, f32[128,4]{0,1:T(4,128)}, u32[]{:S(2)}) copy-start(f32[128,4]{0,1:T(4,128)} %get-tuple-element.121) | copy-start | bytes 6148
  46.7 1.9 %copy-start.13 = (f32[8,128,128]{2,1,0:T(8,128)}, f32[8,128,128]{2,1,0:T(8,128)S(1)}, u32[]{:S(2)}) copy-start(f32[8,128,128]{2,1,0:T(8,128)S(1)} %fusion.41) | copy-start | bytes 1572868
  48.3 1.0 copy-start.17
  49.3 11.3 %copy-start.9 = (f32[1,640,1,256]{3,1,2,0:T(8,128)}, f32[1,640,1,256]{3,1,2,0:T(8,128)S(1)}, u32[]{:S(2)}) copy-start(f32[1,640,1,256]{3,1,2,0:T(8,128)S(1)} %fusion.13) | copy-start | bytes 1966084
  49.3 1.3 copy-start.20
  50.6 1.7 %copy-start.4 = (f32[8,128,128]{2,1,0:T(8,128)}, f32[8,128,128]{2,1,0:T(8,128)S(1)}, u32[]{:S(2)}) copy-start(f32[8,128,128]{2,1,0:T(8,128)S(1)} %convolution_bitcast_fusion.3) | copy-start | bytes 1572868
  53.0 1.3 copy-start.15
  54.3 1.5 copy-start.16
  56.3 7.9 %copy-start.2 = (f32[8,128,128]{2,1,0:T(8,128)}, f32[8,128,128]{2,1,0:T(8,128)S(1)}, u32[]{:S(2)}) copy-start(f32[8,128,128]{2,1,0:T(8,128)S(1)} %get-tuple-element.115) | copy-start | bytes 1572868
  56.3 4.3 %copy-start.18 = (f32[1,640,1,256]{3,1,2,0:T(8,128)S(1)}, f32[1,640,1,256]{3,1,2,0:T(8,128)}, u32[]{:S(2)}) copy-start(f32[1,640,1,256]{3,1,2,0:T(8,128)} %convolution_bitcast_fusion.1) | copy-start | bytes 1966084
  56.4 7.8 %collective-permute-start.5 = (bf16[8,128,128]{2,1,0:T(8,128)(2,1)S(1)}, bf16[8,128,128]{2,1,0:T(8,128)(2,1)S(1)}, u32[]{:S(2)}, u32[]{:S(2)}) collective-permute-start(bf16[8,128,128]{2,1,0:T(8,128)(2,1)S(1)} %get-tuple-element.114), channel_id=1, source_target_pairs={{2,0},{4,2},{6,4},{8,6},{10,8},{12,10},{14,12},{16,14},{18,16},{20... | collective-permute-start | bytes 786440 | tf_op jit(solution)/shard_map/ppermute | solution.py:16
  61.5 8.7 %copy-start.39 = (bf16[128,2048]{1,0:T(8,128)(2,1)S(1)}, bf16[128,2048]{1,0:T(8,128)(2,1)}, u32[]{:S(2)}) copy-start(bf16[128,2048]{1,0:T(8,128)(2,1)} %get-tuple-element.25) | copy-start | bytes 1572868
  65.4 37.4 %collective-permute-start.6 = (bf16[8,128,128]{2,1,0:T(8,128)(2,1)}, bf16[8,128,128]{2,1,0:T(8,128)(2,1)}, u32[]{:S(2)}, u32[]{:S(2)}) collective-permute-start(bf16[8,128,128]{2,1,0:T(8,128)(2,1)} %fusion.26), channel_id=1, source_target_pairs={{2,0},{4,2},{6,4},{8,6},{10,8},{12,10},{14,12},{16,14},{18,16},{20... | collective-permute-start | bytes 786440 | tf_op jit(solution)/shard_map/ppermute | solution.py:16
  73.0 29.8 %copy-start.3 = (f32[8,128,128]{2,1,0:T(8,128)S(1)}, f32[8,128,128]{2,1,0:T(8,128)}, u32[]{:S(2)}) copy-start(f32[8,128,128]{2,1,0:T(8,128)} %copy-done.2) | copy-start | bytes 1572868
  73.0 57.7 %collective-permute-start.4 = (bf16[64,2048]{1,0:T(8,128)(2,1)}, bf16[64,2048]{1,0:T(8,128)(2,1)S(1)}, u32[]{:S(2)}, u32[]{:S(2)}) collective-permute-start(bf16[64,2048]{1,0:T(8,128)(2,1)} %constant_dynamic-slice_fusion), channel_id=1, source_target_pairs={{0,1},{1,0},{2,3},{3,2},{4,5},{5,4},{6,7},{7,6},{8,9},{9,8},{10,11... | collective-permute-start | bytes 786440 | tf_op jit(solution)/shard_map/ppermute | solution.py:217
  89.0 34.1 %collective-permute-start.9 = (bf16[2,128,1,256]{3,1,2,0:T(8,128)(2,1)}, bf16[2,128,1,256]{3,1,2,0:T(8,128)(2,1)S(1)}, u32[]{:S(2)}, u32[]{:S(2)}) collective-permute-start(bf16[2,128,1,256]{3,1,2,0:T(8,128)(2,1)} %get-tuple-element.93), channel_id=1, source_target_pairs={{2,0},{4,2},{6,4},{8,6},{10,8},{12,10},{14,12},{16,14},{18,16},{20... | collective-permute-start | bytes 393224 | tf_op jit(solution)/shard_map/ppermute | solution.py:16
  97.3 27.9 %collective-permute-start.12 = (bf16[2,128,1,256]{3,1,2,0:T(8,128)(2,1)}, bf16[2,128,1,256]{3,1,2,0:T(8,128)(2,1)S(1)}, u32[]{:S(2)}, u32[]{:S(2)}) collective-permute-start(bf16[2,128,1,256]{3,1,2,0:T(8,128)(2,1)} %get-tuple-element.94), channel_id=1, source_target_pairs={{8,0},{10,2},{12,4},{14,6},{16,8},{18,10},{20,12},{22,14},{24,16},... | collective-permute-start | bytes 393224 | tf_op jit(solution)/shard_map/ppermute | solution.py:16
  99.2 26.0 %collective-permute-start.11 = (bf16[2,128,1,256]{3,1,2,0:T(8,128)(2,1)}, bf16[2,128,1,256]{3,1,2,0:T(8,128)(2,1)S(1)}, u32[]{:S(2)}, u32[]{:S(2)}) collective-permute-start(bf16[2,128,1,256]{3,1,2,0:T(8,128)(2,1)} %get-tuple-element.95), channel_id=1, source_target_pairs={{6,0},{8,2},{10,4},{12,6},{14,8},{16,10},{18,12},{20,14},{22,16},{... | collective-permute-start | bytes 393224 | tf_op jit(solution)/shard_map/ppermute | solution.py:16
  102.8 9.4 %copy-start.40 = (bf16[2,128,1,256]{3,1,2,0:T(8,128)(2,1)S(1)}, bf16[2,128,1,256]{3,1,2,0:T(8,128)(2,1)}, u32[]{:S(2)}) copy-start(bf16[2,128,1,256]{3,1,2,0:T(8,128)(2,1)} %get-tuple-element.96) | copy-start | bytes 393220
  104.4 20.9 %copy-start.10 = (f32[1,640,1,256]{3,1,2,0:T(8,128)S(1)}, f32[1,640,1,256]{3,1,2,0:T(8,128)}, u32[]{:S(2)}) copy-start(f32[1,640,1,256]{3,1,2,0:T(8,128)} %copy-done.9) | copy-start | bytes 1966084
  104.4 20.9 %copy-start.19 = (f32[1,640,1,256]{3,1,2,0:T(8,128)S(1)}, f32[1,640,1,256]{3,1,2,0:T(8,128)}, u32[]{:S(2)}) copy-start(f32[1,640,1,256]{3,1,2,0:T(8,128)} %convolution_bitcast_fusion.1) | copy-start | bytes 1966084
  104.4 7.8 %collective-permute-start.7 = (bf16[8,128,128]{2,1,0:T(8,128)(2,1)S(1)}, bf16[8,128,128]{2,1,0:T(8,128)(2,1)S(1)}, u32[]{:S(2)}, u32[]{:S(2)}) collective-permute-start(bf16[8,128,128]{2,1,0:T(8,128)(2,1)S(1)} %fusion.27), channel_id=1, source_target_pairs={{2,0},{4,2},{6,4},{8,6},{10,8},{12,10},{14,12},{16,14},{18,16},{20... | collective-permute-start | bytes 786440 | tf_op jit(solution)/shard_map/ppermute | solution.py:16
  112.2 13.0 %collective-permute-start.10 = (bf16[2,128,1,256]{3,1,2,0:T(8,128)(2,1)S(1)}, bf16[2,128,1,256]{3,1,2,0:T(8,128)(2,1)S(1)}, u32[]{:S(2)}, u32[]{:S(2)}) collective-permute-start(bf16[2,128,1,256]{3,1,2,0:T(8,128)(2,1)S(1)} %copy-done.40), channel_id=1, source_target_pairs={{4,0},{6,2},{8,4},{10,6},{12,8},{14,10},{16,12},{18,14},{20,16},{2... | collective-permute-start | bytes 393224 | tf_op jit(solution)/shard_map/ppermute | solution.py:16
  123.0 7.7 %collective-permute-start.8 = (bf16[8,128,128]{2,1,0:T(8,128)(2,1)S(1)}, bf16[8,128,128]{2,1,0:T(8,128)(2,1)S(1)}, u32[]{:S(2)}, u32[]{:S(2)}) collective-permute-start(bf16[8,128,128]{2,1,0:T(8,128)(2,1)S(1)} %fusion.28), channel_id=1, source_target_pairs={{2,0},{4,2},{6,4},{8,6},{10,8},{12,10},{14,12},{16,14},{18,16},{20... | collective-permute-start | bytes 786440 | tf_op jit(solution)/shard_map/ppermute | solution.py:16
  130.8 1.6 %copy-start.28 = (bf16[64,2048]{1,0:T(8,128)(2,1)}, bf16[64,2048]{1,0:T(8,128)(2,1)S(1)}, u32[]{:S(2)}) copy-start(bf16[64,2048]{1,0:T(8,128)(2,1)S(1)} %collective-permute-done.4) | copy-start | bytes 786436
  137.4 4.2 %copy-start.5 = (f32[8,128,128]{2,1,0:T(8,128)S(1)}, f32[8,128,128]{2,1,0:T(8,128)}, u32[]{:S(2)}) copy-start(f32[8,128,128]{2,1,0:T(8,128)} %copy-done.4) | copy-start | bytes 1572868
  139.5 2.1 %copy-start.11 = (f32[8,128,128]{1,2,0:T(8,128)S(1)}, f32[8,128,128]{1,2,0:T(8,128)}, u32[]{:S(2)}) copy-start(f32[8,128,128]{1,2,0:T(8,128)} %get-tuple-element.117) | copy-start | bytes 1572868
  139.5 2.1 %copy-start.12 = (f32[8,128,128]{2,1,0:T(8,128)S(1)}, f32[8,128,128]{2,1,0:T(8,128)}, u32[]{:S(2)}) copy-start(f32[8,128,128]{2,1,0:T(8,128)} %copy.356) | copy-start | bytes 1572868
  139.5 2.1 %copy-start.14 = (f32[8,128,128]{2,1,0:T(8,128)S(1)}, f32[8,128,128]{2,1,0:T(8,128)}, u32[]{:S(2)}) copy-start(f32[8,128,128]{2,1,0:T(8,128)} %copy-done.13) | copy-start | bytes 1572868
  146.8 1.2 copy-start.8
  147.7 3.8 %copy-start.26 = (f32[128,2048]{1,0:T(8,128)S(1)}, f32[128,2048]{1,0:T(8,128)}, u32[]{:S(2)}) copy-start(f32[128,2048]{1,0:T(8,128)} %get-tuple-element.27) | copy-start | bytes 3145732
  147.8 3.7 %copy-start.29 = (bf16[64,2048]{1,0:T(8,128)(2,1)S(1)}, bf16[64,2048]{1,0:T(8,128)(2,1)}, u32[]{:S(2)}) copy-start(bf16[64,2048]{1,0:T(8,128)(2,1)} %copy-done.28) | copy-start | bytes 786436
where the time goes:
time: 153 us; the launch traced here: 152 us
  starting transfers between devices  64.3 us (42%)
  matrix products  41.7 us (27%)
  local copies, waits for them, and re-layouts  23.8 us (16%)
  other arithmetic  12.1 us (8%)
  waiting for transfers between devices  7.84 us (5%)
  between operations  2.61 us (2%)
    ppermute x12, starting transfers between devices, from_behind(): return lax.ppermute(x, axis, pairs)  50.2 us
    unnamed x101, local copies, waits for them, and re-layouts  17.7 us
    ppermute x1, starting transfers between devices, shards(): received = lax.ppermute(sent, 'head', [(0, 1), (1, 0)])  14.1 us
    ppermute x12, waiting for transfers between devices, from_behind(): return lax.ppermute(x, axis, pairs)  7.84 us
    dot_general x3, matrix products, delta_block(): unit_lower_solve(system - jnp.eye(length, dtype=jnp.float32), inverse, ta...  6.26 us
    dot_general x14, matrix products, matmul(): return jnp.einsum(spec, a, b, precision=lax.Precision.HIGH)  5.99 us
    dot_general x4, matrix products, delta_block(): jnp.einsum('thk,hvk->htv', unit_key, start_state, precision=highest)  3.98 us
    dot_general x3, matrix products, delta_block(): jnp.einsum('thk,hvk->htv', unit_query, start_state, precision=highest)  3.73 us
  transfers between devices with their start and end apart: 13, of which 3 were waited for; matrix products, arithmetic and copies ran while one was open for 23% of the time, Pallas kernels for 0%

commit v1 on v0

--- a/solution.py
+++ b/solution.py
@@ -168,7 +168,6 @@
     inverse = lax.stop_gradient(
         unit_lower_inverse(block_system(key_rows, write_strength, log_decay, segment, repeat))
     )
-    inverse, window_pair = lax.optimization_barrier((inverse, window_pair))
 
     kv_heads = soft_keys.shape[1]
     width = soft_keys.shape[2]

time: 153 us -> 153 us (level)
  no operation moved by 1% of the time
where the time goes in v1:
time: 153 us; the launch traced here: 152 us
  starting transfers between devices  64.3 us (42%)
  matrix products  41.7 us (27%)
  local copies, waits for them, and re-layouts  23.8 us (16%)
  other arithmetic  12.1 us (8%)
  waiting for transfers between devices  7.84 us (5%)
  between operations  2.61 us (2%)
    ppermute x12, starting transfers between devices, from_behind(): return lax.ppermute(x, axis, pairs)  50.2 us
    unnamed x101, local copies, waits for them, and re-layouts  17.7 us
    ppermute x1, starting transfers between devices, shards(): received = lax.ppermute(sent, 'head', [(0, 1), (1, 0)])  14.1 us
    ppermute x12, waiting for transfers between devices, from_behind(): return lax.ppermute(x, axis, pairs)  7.84 us
    dot_general x3, matrix products, delta_block(): unit_lower_solve(system - jnp.eye(length, dtype=jnp.float32), inverse, ta...  6.26 us
    dot_general x14, matrix products, matmul(): return jnp.einsum(spec, a, b, precision=lax.Precision.HIGH)  5.99 us
    dot_general x4, matrix products, delta_block(): jnp.einsum('thk,hvk->htv', unit_key, start_state, precision=highest)  3.98 us
    dot_general x3, matrix products, delta_block(): jnp.einsum('thk,hvk->htv', unit_query, start_state, precision=highest)  3.73 us
  transfers between devices with their start and end apart: 13, of which 3 were waited for; matrix products, arithmetic and copies ran while one was open for 23% of the time, Pallas kernels for 0%

profile of v1, /device:TPU:65, one launch (start us, length us, event | category | flops | bytes accessed | tf_op | source)
XLA Modules:
  0.0 152.3 jit_solution(17004146863409889160)
XLA Ops:
  0.7 1.6 %pad_maximum_fusion.1 = bf16[2,128,1,256]{3,1,2,0:T(8,128)(2,1)} fusion(bf16[1,128,1,256]{3,1,2,0:T(8,128)(2,1)} %bitcast.300, bf16[1,128,1,256]{3,1,2,0:T(8,128)(2,1)} %bitcast.302), kind=kLoop, calls=%fused_computation.197 | loop fusion | flops 65536 | bytes 262144 | tf_op jit(solution)/shard_map/stack | solution.py:160
  2.3 3.7 %collective-permute-start.3 = (bf16[2,128,1,256]{3,1,2,0:T(8,128)(2,1)}, bf16[2,128,1,256]{3,1,2,0:T(8,128)(2,1)}, u32[]{:S(2)}, u32[]{:S(2)}) collective-permute-start(bf16[2,128,1,256]{3,1,2,0:T(8,128)(2,1)} %pad_maximum_fusion.1), channel_id=1, source_target_pairs={{0,2},{2,4},{4,6},{6,8},{8,10},{10,12},{12,14},{14,16},{16,18},{18... | collective-permute-start | bytes 393224 | tf_op jit(solution)/shard_map/ppermute | solution.py:16
  5.9 3.1 %collective-permute-start.2 = (bf16[2,128,1,256]{3,1,2,0:T(8,128)(2,1)}, bf16[2,128,1,256]{3,1,2,0:T(8,128)(2,1)}, u32[]{:S(2)}, u32[]{:S(2)}) collective-permute-start(bf16[2,128,1,256]{3,1,2,0:T(8,128)(2,1)} %pad_maximum_fusion.1), channel_id=1, source_target_pairs={{0,4},{2,6},{4,8},{6,10},{8,12},{10,14},{12,16},{14,18},{16,20},{1... | collective-permute-start | bytes 393224 | tf_op jit(solution)/shard_map/ppermute | solution.py:16
  9.1 3.4 %collective-permute-start.1 = (bf16[2,128,1,256]{3,1,2,0:T(8,128)(2,1)}, bf16[2,128,1,256]{3,1,2,0:T(8,128)(2,1)}, u32[]{:S(2)}, u32[]{:S(2)}) collective-permute-start(bf16[2,128,1,256]{3,1,2,0:T(8,128)(2,1)} %pad_maximum_fusion.1), channel_id=1, source_target_pairs={{0,6},{2,8},{4,10},{6,12},{8,14},{10,16},{12,18},{14,20},{16,22},{... | collective-permute-start | bytes 393224 | tf_op jit(solution)/shard_map/ppermute | solution.py:16
  12.5 3.4 %collective-permute-start = (bf16[2,128,1,256]{3,1,2,0:T(8,128)(2,1)}, bf16[2,128,1,256]{3,1,2,0:T(8,128)(2,1)}, u32[]{:S(2)}, u32[]{:S(2)}) collective-permute-start(bf16[2,128,1,256]{3,1,2,0:T(8,128)(2,1)} %pad_maximum_fusion.1), channel_id=1, source_target_pairs={{0,8},{2,10},{4,12},{6,14},{8,16},{10,18},{12,20},{14,22},{16,24},... | collective-permute-start | bytes 393224 | tf_op jit(solution)/shard_map/ppermute | solution.py:16
  16.1 0.7 pad_bitcast_fusion
  17.5 1.3 fusion.142
  19.8 0.8 copy.326
  22.6 0.9 compare_and_fusion
  23.4 1.0 copy.336
  25.0 0.7 fusion.20
  31.1 0.8 copy_convert_fusion
  31.9 1.3 fusion.32
  33.2 0.9 copy.333
  34.1 0.9 copy.329
  35.0 0.9 constant_dynamic-update-slice_fusion.4
  36.0 0.9 constant_dynamic-update-slice_fusion.3
  36.9 0.9 constant_dynamic-update-slice_fusion.2
  37.8 0.9 constant_dynamic-update-slice_fusion.1
  38.8 1.5 fusion.170
  40.6 1.0 fusion.38
  41.6 1.3 convolution_bitcast_fusion.1
  43.0 2.7 %fusion.171 = (bf16[128,2048]{1,0:T(8,128)(2,1)}, f32[128,2048]{1,0:T(8,128)}) fusion(bf16[2048,4,256]{2,1,0:T(4,128)(2,1)S(1)} %copy-done.41, f32[128,1,4,256]{0,3,2,1:T(8,128)S(1)} %get-tuple-element.118, bf16[128,4,256]{0,2,1:T(8,128)(2,1)S(1)} %copy-done.34, bf16[128,4,256]{0,2,1:T(8,128)(2,1)S(1)} %copy-done.32), kind=kOutput, calls=%fused_computation.329 | convolution fusion | flops 538443776 | bytes 6815744 | tf_op jit(solution)/shard_map/dot_general | solution.py:205
  46.7 0.7 fusion.16
  48.6 0.7 copy-done.17
  49.3 0.9 fusion.52
  51.3 1.0 multiply_multiply_fusion
  53.0 0.8 convolution_add_fusion.2
  55.0 0.8 fusion.18
  56.4 3.3 %collective-permute-start.5 = (bf16[8,128,128]{2,1,0:T(8,128)(2,1)S(1)}, bf16[8,128,128]{2,1,0:T(8,128)(2,1)S(1)}, u32[]{:S(2)}, u32[]{:S(2)}) collective-permute-start(bf16[8,128,128]{2,1,0:T(8,128)(2,1)S(1)} %get-tuple-element.110), channel_id=1, source_target_pairs={{2,0},{4,2},{6,4},{8,6},{10,8},{12,10},{14,12},{16,14},{18,16},{20... | collective-permute-start | bytes 786440 | tf_op jit(solution)/shard_map/ppermute | solution.py:16
  60.8 0.8 fusion.169
  61.5 1.2 fusion.14
  62.8 1.4 collective-permute-done.5
  64.2 1.2 fusion.26
  65.4 4.8 %collective-permute-start.6 = (bf16[8,128,128]{2,1,0:T(8,128)(2,1)}, bf16[8,128,128]{2,1,0:T(8,128)(2,1)}, u32[]{:S(2)}, u32[]{:S(2)}) collective-permute-start(bf16[8,128,128]{2,1,0:T(8,128)(2,1)} %fusion.26), channel_id=1, source_target_pairs={{2,0},{4,2},{6,4},{8,6},{10,8},{12,10},{14,12},{16,14},{18,16},{20... | collective-permute-start | bytes 786440 | tf_op jit(solution)/shard_map/ppermute | solution.py:16
  70.3 0.7 constant_dynamic-slice_fusion
  71.0 2.0 %copy.384 = f32[128,4,256]{2,1,0:T(4,128)} copy(f32[128,4,256]{0,2,1:T(8,128)} %fusion.14) | data formatting | bytes 1048576
  73.0 14.1 %collective-permute-start.4 = (bf16[64,2048]{1,0:T(8,128)(2,1)}, bf16[64,2048]{1,0:T(8,128)(2,1)S(1)}, u32[]{:S(2)}, u32[]{:S(2)}) collective-permute-start(bf16[64,2048]{1,0:T(8,128)(2,1)} %constant_dynamic-slice_fusion), channel_id=1, source_target_pairs={{0,1},{1,0},{2,3},{3,2},{4,5},{5,4},{6,7},{7,6},{8,9},{9,8},{10,11... | collective-permute-start | bytes 786440 | tf_op jit(solution)/shard_map/ppermute | solution.py:216
  87.1 1.8 %copy.380 = f32[128,4,128]{2,1,0:T(4,128)} copy(f32[128,4,128]{2,0,1:T(8,128)} %get-tuple-element.96) | data formatting | bytes 524288
  89.0 8.3 %collective-permute-start.9 = (bf16[2,128,1,256]{3,1,2,0:T(8,128)(2,1)}, bf16[2,128,1,256]{3,1,2,0:T(8,128)(2,1)S(1)}, u32[]{:S(2)}, u32[]{:S(2)}) collective-permute-start(bf16[2,128,1,256]{3,1,2,0:T(8,128)(2,1)} %get-tuple-element.89), channel_id=1, source_target_pairs={{2,0},{4,2},{6,4},{8,6},{10,8},{12,10},{14,12},{16,14},{18,16},{20... | collective-permute-start | bytes 393224 | tf_op jit(solution)/shard_map/ppermute | solution.py:16
  97.3 1.9 %collective-permute-start.12 = (bf16[2,128,1,256]{3,1,2,0:T(8,128)(2,1)}, bf16[2,128,1,256]{3,1,2,0:T(8,128)(2,1)S(1)}, u32[]{:S(2)}, u32[]{:S(2)}) collective-permute-start(bf16[2,128,1,256]{3,1,2,0:T(8,128)(2,1)} %get-tuple-element.90), channel_id=1, source_target_pairs={{8,0},{10,2},{12,4},{14,6},{16,8},{18,10},{20,12},{22,14},{24,16},... | collective-permute-start | bytes 393224 | tf_op jit(solution)/shard_map/ppermute | solution.py:16
  99.2 1.9 %collective-permute-start.11 = (bf16[2,128,1,256]{3,1,2,0:T(8,128)(2,1)}, bf16[2,128,1,256]{3,1,2,0:T(8,128)(2,1)S(1)}, u32[]{:S(2)}, u32[]{:S(2)}) collective-permute-start(bf16[2,128,1,256]{3,1,2,0:T(8,128)(2,1)} %get-tuple-element.91), channel_id=1, source_target_pairs={{6,0},{8,2},{10,4},{12,6},{14,8},{16,10},{18,12},{20,14},{22,16},{... | collective-permute-start | bytes 393224 | tf_op jit(solution)/shard_map/ppermute | solution.py:16
  101.1 1.7 %fusion.29 = f32[8,128]{1,0:T(8,128)S(1)} fusion(f32[128,8,128]{2,0,1:T(8,128)S(1)} %bitcast.281, f32[1,8,128,128]{3,2,1,0:T(8,128)S(1)} %copy-done.1, bf16[128,8,128]{2,1,0:T(8,128)(2,1)} %param.21), kind=kOutput, calls=%fused_computation.64 | convolution fusion | flops 101055488 | bytes 1314816 | tf_op jit(solution)/shard_map/jvp(thk,hvk->htv)/dot_general | solution.py:116
  102.9 1.5 fusion.27
  104.4 3.8 %collective-permute-start.7 = (bf16[8,128,128]{2,1,0:T(8,128)(2,1)S(1)}, bf16[8,128,128]{2,1,0:T(8,128)(2,1)S(1)}, u32[]{:S(2)}, u32[]{:S(2)}) collective-permute-start(bf16[8,128,128]{2,1,0:T(8,128)(2,1)S(1)} %fusion.27), channel_id=1, source_target_pairs={{2,0},{4,2},{6,4},{8,6},{10,8},{12,10},{14,12},{16,14},{18,16},{20... | collective-permute-start | bytes 786440 | tf_op jit(solution)/shard_map/ppermute | solution.py:16
  108.1 1.5 fusion.174
  109.6 2.6 %collective-permute-done.7 = bf16[8,128,128]{2,1,0:T(8,128)(2,1)S(1)} collective-permute-done((bf16[8,128,128]{2,1,0:T(8,128)(2,1)S(1)}, bf16[8,128,128]{2,1,0:T(8,128)(2,1)S(1)}, u32[]{:S(2)}, u32[]{:S(2)}) %collective-permute-start.7) | collective-permute-done | bytes 262176 | tf_op jit(solution)/shard_map/ppermute | solution.py:16
  112.2 10.3 %collective-permute-start.10 = (bf16[2,128,1,256]{3,1,2,0:T(8,128)(2,1)S(1)}, bf16[2,128,1,256]{3,1,2,0:T(8,128)(2,1)S(1)}, u32[]{:S(2)}, u32[]{:S(2)}) collective-permute-start(bf16[2,128,1,256]{3,1,2,0:T(8,128)(2,1)S(1)} %copy-done.40), channel_id=1, source_target_pairs={{4,0},{6,2},{8,4},{10,6},{12,8},{14,10},{16,12},{18,14},{20,16},{2... | collective-permute-start | bytes 393224 | tf_op jit(solution)/shard_map/ppermute | solution.py:16
  123.0 2.1 %collective-permute-start.8 = (bf16[8,128,128]{2,1,0:T(8,128)(2,1)S(1)}, bf16[8,128,128]{2,1,0:T(8,128)(2,1)S(1)}, u32[]{:S(2)}, u32[]{:S(2)}) collective-permute-start(bf16[8,128,128]{2,1,0:T(8,128)(2,1)S(1)} %fusion.28), channel_id=1, source_target_pairs={{2,0},{4,2},{6,4},{8,6},{10,8},{12,10},{14,12},{16,14},{18,16},{20... | collective-permute-start | bytes 786440 | tf_op jit(solution)/shard_map/ppermute | solution.py:16
  125.4 0.8 copy.386
  126.2 0.8 copy.385
  126.9 3.8 %collective-permute-done.8 = bf16[8,128,128]{2,1,0:T(8,128)(2,1)S(1)} collective-permute-done((bf16[8,128,128]{2,1,0:T(8,128)(2,1)S(1)}, bf16[8,128,128]{2,1,0:T(8,128)(2,1)S(1)}, u32[]{:S(2)}, u32[]{:S(2)}) %collective-permute-start.8) | collective-permute-done | bytes 262176 | tf_op jit(solution)/shard_map/ppermute | solution.py:16
  131.0 1.5 multiply_reduce_fusion.1
  132.5 2.5 %bitcast_multiply_fusion = (f32[128,8,128]{0,2,1:T(8,128)}, f32[8,128,128]{1,2,0:T(8,128)}) fusion(f32[128,8]{0,1:T(8,128)S(1)} %copy-done.23, f32[8,128,128]{2,1,0:T(8,128)S(1)} %convolution_subtract_fusion, f32[8,128,128]{1,2,0:T(8,128)} %copy-done.16, f32[8,128,128]{1,2,0:T(8,128)} %get-tuple-element.116, f32[8,128]{1,0:T(8,128)S(1)} %get-tuple-element.99), kind=kOutput, calls=%fused_computation.79 | convolution fusion | flops 101056512 | bytes 2629632 | tf_op jit(solution)/shard_map/transpose(jvp(hst,hsv->htv))/dot_general | solution.py:115
  135.1 2.0 %copy.382 = f32[128,8,128]{2,1,0:T(8,128)} copy(f32[128,8,128]{0,2,1:T(8,128)} %get-tuple-element.112) | data formatting | bytes 1048576
  137.4 2.1 %copy.356 = f32[8,128,128]{2,1,0:T(8,128)} copy(f32[8,128,128]{1,2,0:T(8,128)} %get-tuple-element.113) | data formatting | bytes 1048576 | tf_op jit(solution)/shard_map/transpose(jvp(hst,hsv->htv))/dot_general | solution.py:115
  139.5 2.0 %convolution_bitcast_fusion.7 = f32[128,8,128]{0,2,1:T(8,128)S(1)} fusion(f32[1,8,128,128]{3,2,1,0:T(8,128)S(1)} %copy-done.1, f32[8,128,128]{2,1,0:T(8,128)} %copy.356, f32[8,128]{1,0:T(8,128)S(1)} %bitcast.296, f32[8,128]{1,0:T(8,128)S(1)} %get-tuple-element.100), kind=kOutput, calls=%fused_computation.54 | convolution fusion | flops 101056512 | bytes 1581056 | tf_op jit(solution)/shard_map/transpose(jvp(thk,hvk->htv))/dot_general | solution.py:111
  141.6 3.0 %multiply_select_fusion = (f32[8,128,128]{2,1,0:T(8,128)S(1)}, f32[8,128]{1,0:T(8,128)S(1)}, f32[8,128]{1,0:T(8,128)S(1)}, f32[8,128]{1,0:T(8,128)S(1)}, f32[8,128,128]{2,1,0:T(8,128)S(1)}) fusion(f32[8,128,128]{2,1,0:T(8,128)} %fusion.174, f32[8,128,128]{2,1,0:T(8,128)} %copy-done.15, f32[8,128,128]{2,1,0:T(8,128)S(1)} %copy-done.5, ...), kind=kOutput, calls=%fused_computation.90 | convolution fusion | flops 103674880 | bytes 5300224 | tf_op jit(solution)/shard_map/transpose(jvp(htv,hsv->hts))/dot_general | solution.py:115
  145.1 0.8 fusion.24
  145.9 0.9 fusion.22
  146.8 0.9 bitcast_reduce_fusion.1
  148.1 0.8 copy.381
  149.1 1.1 reduce_window_sum.44
  151.5 0.8 convert_add_fusion
  (193 shorter events, 19.2 us)
Async XLA Ops:
  0.6 38.2 %copy-start = (bf16[128,4,256]{2,1,0:T(4,128)(2,1)S(1)}, bf16[128,4,256]{2,1,0:T(4,128)(2,1)}, u32[]{:S(2)}) copy-start(bf16[128,4,256]{2,1,0:T(4,128)(2,1)} %param.22) | copy-start | bytes 786436
  0.7 24.0 %copy-start.38 = (bf16[128,4,128]{2,1,0:T(4,128)(2,1)S(1)}, bf16[128,4,128]{2,1,0:T(4,128)(2,1)}, u32[]{:S(2)}) copy-start(bf16[128,4,128]{2,1,0:T(4,128)(2,1)} %param.15) | copy-start | bytes 393220
  2.3 35.6 %collective-permute-start.3 = (bf16[2,128,1,256]{3,1,2,0:T(8,128)(2,1)}, bf16[2,128,1,256]{3,1,2,0:T(8,128)(2,1)}, u32[]{:S(2)}, u32[]{:S(2)}) collective-permute-start(bf16[2,128,1,256]{3,1,2,0:T(8,128)(2,1)} %pad_maximum_fusion.1), channel_id=1, source_target_pairs={{0,2},{2,4},{4,6},{6,8},{8,10},{10,12},{12,14},{14,16},{16,18},{18... | collective-permute-start | bytes 393224 | tf_op jit(solution)/shard_map/ppermute | solution.py:16
  5.9 30.9 %collective-permute-start.2 = (bf16[2,128,1,256]{3,1,2,0:T(8,128)(2,1)}, bf16[2,128,1,256]{3,1,2,0:T(8,128)(2,1)}, u32[]{:S(2)}, u32[]{:S(2)}) collective-permute-start(bf16[2,128,1,256]{3,1,2,0:T(8,128)(2,1)} %pad_maximum_fusion.1), channel_id=1, source_target_pairs={{0,4},{2,6},{4,8},{6,10},{8,12},{10,14},{12,16},{14,18},{16,20},{1... | collective-permute-start | bytes 393224 | tf_op jit(solution)/shard_map/ppermute | solution.py:16
  9.1 26.9 %collective-permute-start.1 = (bf16[2,128,1,256]{3,1,2,0:T(8,128)(2,1)}, bf16[2,128,1,256]{3,1,2,0:T(8,128)(2,1)}, u32[]{:S(2)}, u32[]{:S(2)}) collective-permute-start(bf16[2,128,1,256]{3,1,2,0:T(8,128)(2,1)} %pad_maximum_fusion.1), channel_id=1, source_target_pairs={{0,6},{2,8},{4,10},{6,12},{8,14},{10,16},{12,18},{14,20},{16,22},{... | collective-permute-start | bytes 393224 | tf_op jit(solution)/shard_map/ppermute | solution.py:16
  12.5 22.5 %collective-permute-start = (bf16[2,128,1,256]{3,1,2,0:T(8,128)(2,1)}, bf16[2,128,1,256]{3,1,2,0:T(8,128)(2,1)}, u32[]{:S(2)}, u32[]{:S(2)}) collective-permute-start(bf16[2,128,1,256]{3,1,2,0:T(8,128)(2,1)} %pad_maximum_fusion.1), channel_id=1, source_target_pairs={{0,8},{2,10},{4,12},{6,14},{8,16},{10,18},{12,20},{14,22},{16,24},... | collective-permute-start | bytes 393224 | tf_op jit(solution)/shard_map/ppermute | solution.py:16
  22.6 2.4 %copy-start.23 = (f32[128,8]{0,1:T(8,128)S(1)}, f32[128,8]{0,1:T(8,128)}, u32[]{:S(2)}) copy-start(f32[128,8]{0,1:T(8,128)} %param.18) | copy-start | bytes 12292
  30.1 1.0 copy-start.27
  30.5 1.4 copy-start.1
  30.5 1.4 copy-start.6
  31.1 2.1 %copy-start.30 = (bf16[128,4,256]{2,1,0:T(4,128)(2,1)S(1)}, bf16[128,4,256]{2,1,0:T(4,128)(2,1)}, u32[]{:S(2)}) copy-start(bf16[128,4,256]{2,1,0:T(4,128)(2,1)} %param.25) | copy-start | bytes 786436
  31.9 2.2 %copy-start.31 = (bf16[128,4,256]{2,1,0:T(4,128)(2,1)S(1)}, bf16[128,4,256]{2,1,0:T(4,128)(2,1)}, u32[]{:S(2)}) copy-start(bf16[128,4,256]{2,1,0:T(4,128)(2,1)} %param.26) | copy-start | bytes 786436
  33.2 5.6 %copy-start.36 = (bf16[128,1,256]{2,0,1:T(8,128)(2,1)S(1)}, bf16[128,1,256]{2,0,1:T(8,128)(2,1)}, u32[]{:S(2)}) copy-start(bf16[128,1,256]{2,0,1:T(8,128)(2,1)} %param.24) | copy-start | bytes 196612
  33.2 5.6 %copy-start.37 = (bf16[128,1,256]{2,0,1:T(8,128)(2,1)S(1)}, bf16[128,1,256]{2,0,1:T(8,128)(2,1)}, u32[]{:S(2)}) copy-start(bf16[128,1,256]{2,0,1:T(8,128)(2,1)} %param.23) | copy-start | bytes 196612
  33.2 12.5 %copy-start.7 = (f32[128,4,128]{0,2,1:T(8,128)}, f32[128,4,128]{0,2,1:T(8,128)S(1)}, u32[]{:S(2)}) copy-start(f32[128,4,128]{0,2,1:T(8,128)S(1)} %convert_element_type.116) | copy-start | bytes 786436
  38.8 1.7 %copy-start.24 = (bf16[2,640,1,256]{3,1,2,0:T(8,128)(2,1)}, bf16[2,640,1,256]{3,1,2,0:T(8,128)(2,1)S(1)}, u32[]{:S(2)}) copy-start(bf16[2,640,1,256]{3,1,2,0:T(8,128)(2,1)S(1)} %constant_dynamic-update-slice_fusion) | copy-start | bytes 1966084
  38.8 1.7 %copy-start.32 = (bf16[128,4,256]{0,2,1:T(8,128)(2,1)S(1)}, bf16[128,4,256]{0,2,1:T(8,128)(2,1)}, u32[]{:S(2)}) copy-start(bf16[128,4,256]{0,2,1:T(8,128)(2,1)} %copy.333) | copy-start | bytes 786436
  38.8 1.7 %copy-start.34 = (bf16[128,4,256]{0,2,1:T(8,128)(2,1)S(1)}, bf16[128,4,256]{0,2,1:T(8,128)(2,1)}, u32[]{:S(2)}) copy-start(bf16[128,4,256]{0,2,1:T(8,128)(2,1)} %copy.329) | copy-start | bytes 786436
  40.3 1.3 copy-start.21
  40.6 2.4 %copy-start.41 = (bf16[2048,4,256]{2,1,0:T(4,128)(2,1)S(1)}, bf16[2048,4,256]{2,1,0:T(4,128)(2,1)}, u32[]{:S(2)}) copy-start(bf16[2048,4,256]{2,1,0:T(4,128)(2,1)} %param.27) | copy-start | bytes 12582916
  46.0 1.4 copy-start.22
  46.0 1.5 copy-start.25
  46.0 1.5 copy-start.33
  46.0 1.6 %copy-start.35 = (bf16[128,4,256]{0,2,1:T(8,128)(2,1)S(1)}, bf16[128,4,256]{0,2,1:T(8,128)(2,1)}, u32[]{:S(2)}) copy-start(bf16[128,4,256]{0,2,1:T(8,128)(2,1)} %copy.329) | copy-start | bytes 786436
  46.0 1.6 %copy-start.42 = (f32[128,4]{0,1:T(4,128)S(1)}, f32[128,4]{0,1:T(4,128)}, u32[]{:S(2)}) copy-start(f32[128,4]{0,1:T(4,128)} %get-tuple-element.117) | copy-start | bytes 6148
  46.7 1.9 %copy-start.13 = (f32[8,128,128]{2,1,0:T(8,128)}, f32[8,128,128]{2,1,0:T(8,128)S(1)}, u32[]{:S(2)}) copy-start(f32[8,128,128]{2,1,0:T(8,128)S(1)} %fusion.41) | copy-start | bytes 1572868
  48.3 1.0 copy-start.17
  49.3 11.3 %copy-start.9 = (f32[1,640,1,256]{3,1,2,0:T(8,128)}, f32[1,640,1,256]{3,1,2,0:T(8,128)S(1)}, u32[]{:S(2)}) copy-start(f32[1,640,1,256]{3,1,2,0:T(8,128)S(1)} %fusion.13) | copy-start | bytes 1966084
  49.3 1.3 copy-start.20
  50.6 1.7 %copy-start.4 = (f32[8,128,128]{2,1,0:T(8,128)}, f32[8,128,128]{2,1,0:T(8,128)S(1)}, u32[]{:S(2)}) copy-start(f32[8,128,128]{2,1,0:T(8,128)S(1)} %convolution_bitcast_fusion.3) | copy-start | bytes 1572868
  53.0 1.3 copy-start.15
  54.3 1.5 copy-start.16
  56.3 7.9 %copy-start.2 = (f32[8,128,128]{2,1,0:T(8,128)}, f32[8,128,128]{2,1,0:T(8,128)S(1)}, u32[]{:S(2)}) copy-start(f32[8,128,128]{2,1,0:T(8,128)S(1)} %get-tuple-element.111) | copy-start | bytes 1572868
  56.3 4.3 %copy-start.18 = (f32[1,640,1,256]{3,1,2,0:T(8,128)S(1)}, f32[1,640,1,256]{3,1,2,0:T(8,128)}, u32[]{:S(2)}) copy-start(f32[1,640,1,256]{3,1,2,0:T(8,128)} %convolution_bitcast_fusion.1) | copy-start | bytes 1966084
  56.4 7.8 %collective-permute-start.5 = (bf16[8,128,128]{2,1,0:T(8,128)(2,1)S(1)}, bf16[8,128,128]{2,1,0:T(8,128)(2,1)S(1)}, u32[]{:S(2)}, u32[]{:S(2)}) collective-permute-start(bf16[8,128,128]{2,1,0:T(8,128)(2,1)S(1)} %get-tuple-element.110), channel_id=1, source_target_pairs={{2,0},{4,2},{6,4},{8,6},{10,8},{12,10},{14,12},{16,14},{18,16},{20... | collective-permute-start | bytes 786440 | tf_op jit(solution)/shard_map/ppermute | solution.py:16
  61.5 8.7 %copy-start.39 = (bf16[128,2048]{1,0:T(8,128)(2,1)S(1)}, bf16[128,2048]{1,0:T(8,128)(2,1)}, u32[]{:S(2)}) copy-start(bf16[128,2048]{1,0:T(8,128)(2,1)} %get-tuple-element.21) | copy-start | bytes 1572868
  65.4 37.4 %collective-permute-start.6 = (bf16[8,128,128]{2,1,0:T(8,128)(2,1)}, bf16[8,128,128]{2,1,0:T(8,128)(2,1)}, u32[]{:S(2)}, u32[]{:S(2)}) collective-permute-start(bf16[8,128,128]{2,1,0:T(8,128)(2,1)} %fusion.26), channel_id=1, source_target_pairs={{2,0},{4,2},{6,4},{8,6},{10,8},{12,10},{14,12},{16,14},{18,16},{20... | collective-permute-start | bytes 786440 | tf_op jit(solution)/shard_map/ppermute | solution.py:16
  73.0 29.8 %copy-start.3 = (f32[8,128,128]{2,1,0:T(8,128)S(1)}, f32[8,128,128]{2,1,0:T(8,128)}, u32[]{:S(2)}) copy-start(f32[8,128,128]{2,1,0:T(8,128)} %copy-done.2) | copy-start | bytes 1572868
  73.0 57.7 %collective-permute-start.4 = (bf16[64,2048]{1,0:T(8,128)(2,1)}, bf16[64,2048]{1,0:T(8,128)(2,1)S(1)}, u32[]{:S(2)}, u32[]{:S(2)}) collective-permute-start(bf16[64,2048]{1,0:T(8,128)(2,1)} %constant_dynamic-slice_fusion), channel_id=1, source_target_pairs={{0,1},{1,0},{2,3},{3,2},{4,5},{5,4},{6,7},{7,6},{8,9},{9,8},{10,11... | collective-permute-start | bytes 786440 | tf_op jit(solution)/shard_map/ppermute | solution.py:216
  89.0 34.1 %collective-permute-start.9 = (bf16[2,128,1,256]{3,1,2,0:T(8,128)(2,1)}, bf16[2,128,1,256]{3,1,2,0:T(8,128)(2,1)S(1)}, u32[]{:S(2)}, u32[]{:S(2)}) collective-permute-start(bf16[2,128,1,256]{3,1,2,0:T(8,128)(2,1)} %get-tuple-element.89), channel_id=1, source_target_pairs={{2,0},{4,2},{6,4},{8,6},{10,8},{12,10},{14,12},{16,14},{18,16},{20... | collective-permute-start | bytes 393224 | tf_op jit(solution)/shard_map/ppermute | solution.py:16
  97.3 27.9 %collective-permute-start.12 = (bf16[2,128,1,256]{3,1,2,0:T(8,128)(2,1)}, bf16[2,128,1,256]{3,1,2,0:T(8,128)(2,1)S(1)}, u32[]{:S(2)}, u32[]{:S(2)}) collective-permute-start(bf16[2,128,1,256]{3,1,2,0:T(8,128)(2,1)} %get-tuple-element.90), channel_id=1, source_target_pairs={{8,0},{10,2},{12,4},{14,6},{16,8},{18,10},{20,12},{22,14},{24,16},... | collective-permute-start | bytes 393224 | tf_op jit(solution)/shard_map/ppermute | solution.py:16
  99.2 26.0 %collective-permute-start.11 = (bf16[2,128,1,256]{3,1,2,0:T(8,128)(2,1)}, bf16[2,128,1,256]{3,1,2,0:T(8,128)(2,1)S(1)}, u32[]{:S(2)}, u32[]{:S(2)}) collective-permute-start(bf16[2,128,1,256]{3,1,2,0:T(8,128)(2,1)} %get-tuple-element.91), channel_id=1, source_target_pairs={{6,0},{8,2},{10,4},{12,6},{14,8},{16,10},{18,12},{20,14},{22,16},{... | collective-permute-start | bytes 393224 | tf_op jit(solution)/shard_map/ppermute | solution.py:16
  102.8 9.4 %copy-start.40 = (bf16[2,128,1,256]{3,1,2,0:T(8,128)(2,1)S(1)}, bf16[2,128,1,256]{3,1,2,0:T(8,128)(2,1)}, u32[]{:S(2)}) copy-start(bf16[2,128,1,256]{3,1,2,0:T(8,128)(2,1)} %get-tuple-element.92) | copy-start | bytes 393220
  104.4 20.9 %copy-start.10 = (f32[1,640,1,256]{3,1,2,0:T(8,128)S(1)}, f32[1,640,1,256]{3,1,2,0:T(8,128)}, u32[]{:S(2)}) copy-start(f32[1,640,1,256]{3,1,2,0:T(8,128)} %copy-done.9) | copy-start | bytes 1966084
  104.4 20.9 %copy-start.19 = (f32[1,640,1,256]{3,1,2,0:T(8,128)S(1)}, f32[1,640,1,256]{3,1,2,0:T(8,128)}, u32[]{:S(2)}) copy-start(f32[1,640,1,256]{3,1,2,0:T(8,128)} %convolution_bitcast_fusion.1) | copy-start | bytes 1966084
  104.4 7.8 %collective-permute-start.7 = (bf16[8,128,128]{2,1,0:T(8,128)(2,1)S(1)}, bf16[8,128,128]{2,1,0:T(8,128)(2,1)S(1)}, u32[]{:S(2)}, u32[]{:S(2)}) collective-permute-start(bf16[8,128,128]{2,1,0:T(8,128)(2,1)S(1)} %fusion.27), channel_id=1, source_target_pairs={{2,0},{4,2},{6,4},{8,6},{10,8},{12,10},{14,12},{16,14},{18,16},{20... | collective-permute-start | bytes 786440 | tf_op jit(solution)/shard_map/ppermute | solution.py:16
  112.2 13.0 %collective-permute-start.10 = (bf16[2,128,1,256]{3,1,2,0:T(8,128)(2,1)S(1)}, bf16[2,128,1,256]{3,1,2,0:T(8,128)(2,1)S(1)}, u32[]{:S(2)}, u32[]{:S(2)}) collective-permute-start(bf16[2,128,1,256]{3,1,2,0:T(8,128)(2,1)S(1)} %copy-done.40), channel_id=1, source_target_pairs={{4,0},{6,2},{8,4},{10,6},{12,8},{14,10},{16,12},{18,14},{20,16},{2... | collective-permute-start | bytes 393224 | tf_op jit(solution)/shard_map/ppermute | solution.py:16
  123.0 7.7 %collective-permute-start.8 = (bf16[8,128,128]{2,1,0:T(8,128)(2,1)S(1)}, bf16[8,128,128]{2,1,0:T(8,128)(2,1)S(1)}, u32[]{:S(2)}, u32[]{:S(2)}) collective-permute-start(bf16[8,128,128]{2,1,0:T(8,128)(2,1)S(1)} %fusion.28), channel_id=1, source_target_pairs={{2,0},{4,2},{6,4},{8,6},{10,8},{12,10},{14,12},{16,14},{18,16},{20... | collective-permute-start | bytes 786440 | tf_op jit(solution)/shard_map/ppermute | solution.py:16
  130.8 1.6 %copy-start.28 = (bf16[64,2048]{1,0:T(8,128)(2,1)}, bf16[64,2048]{1,0:T(8,128)(2,1)S(1)}, u32[]{:S(2)}) copy-start(bf16[64,2048]{1,0:T(8,128)(2,1)S(1)} %collective-permute-done.4) | copy-start | bytes 786436
  137.4 4.2 %copy-start.5 = (f32[8,128,128]{2,1,0:T(8,128)S(1)}, f32[8,128,128]{2,1,0:T(8,128)}, u32[]{:S(2)}) copy-start(f32[8,128,128]{2,1,0:T(8,128)} %copy-done.4) | copy-start | bytes 1572868
  139.5 2.1 %copy-start.11 = (f32[8,128,128]{1,2,0:T(8,128)S(1)}, f32[8,128,128]{1,2,0:T(8,128)}, u32[]{:S(2)}) copy-start(f32[8,128,128]{1,2,0:T(8,128)} %get-tuple-element.113) | copy-start | bytes 1572868
  139.5 2.1 %copy-start.12 = (f32[8,128,128]{2,1,0:T(8,128)S(1)}, f32[8,128,128]{2,1,0:T(8,128)}, u32[]{:S(2)}) copy-start(f32[8,128,128]{2,1,0:T(8,128)} %copy.356) | copy-start | bytes 1572868
  139.5 2.1 %copy-start.14 = (f32[8,128,128]{2,1,0:T(8,128)S(1)}, f32[8,128,128]{2,1,0:T(8,128)}, u32[]{:S(2)}) copy-start(f32[8,128,128]{2,1,0:T(8,128)} %copy-done.13) | copy-start | bytes 1572868
  146.8 1.2 copy-start.8
  147.7 3.8 %copy-start.26 = (f32[128,2048]{1,0:T(8,128)S(1)}, f32[128,2048]{1,0:T(8,128)}, u32[]{:S(2)}) copy-start(f32[128,2048]{1,0:T(8,128)} %get-tuple-element.23) | copy-start | bytes 3145732
  147.8 3.7 %copy-start.29 = (bf16[64,2048]{1,0:T(8,128)(2,1)S(1)}, bf16[64,2048]{1,0:T(8,128)(2,1)}, u32[]{:S(2)}) copy-start(bf16[64,2048]{1,0:T(8,128)(2,1)} %copy-done.28) | copy-start | bytes 786436
